TPU v7x, 512 devices: a whole 4x8x8 slice. The times are simulated.
512 devices in a mesh: owner: 16 (over x, y_hi), beam: 32 (over y_lo, z, core).
Axes of the slice: x: 4, y: 8 (y_hi: 4, y_lo: 2; y = y_hi * 2 + y_lo), z: 8, core: 2. Of those that a mesh axis runs over, the one named last changes fastest.
Arguments:
- hidden: bfloat16 [4096, 8192], P('owner'), may hold values from -6 to 6
- norm_gain: bfloat16 [8192], replicated, may hold values from 0.099609375 to 1.8984375
- w_qkv: bfloat16 [8192, 10240], P('owner', 'beam'), may hold values from -0.0625 to 0.0625
- w_out: bfloat16 [8192, 8192], P('beam', 'owner'), may hold values from -0.125 to 0.125
- kv_cache: bfloat16 [16384, 2, 8, 1024], P(('owner', 'beam')), may hold values from -384 to 384
- lengths: int32 [4096], P('owner'), may hold values from 1 to 32, 98304 in all
- kept_parent_device: int32 [16384, 1], P('owner'), may hold values from 0 to 31; in each aligned block of 32 rows (0 to 31, 32 to 63, ...) at most 2 rows name the same one
- keep_block: int32 [16384], P('owner'), may hold values from 0 to 31
Outputs:
- mixed: bfloat16 [4096, 8192], P('owner', 'beam')
Inputs may be any that keep to these rules, and one draw needn't show every extreme that they name: `kept_parent_device`: in each aligned block of 32 entries (the new blocks of one device) no value appears more than 2 times, and some value appears exactly 2 times in some block. `lengths`: each entry is at least 1; the largest is exactly 32.
All inputs are finite; a program needn't handle non-finite values. No bound on the sum of `lengths` on one device may be relied on, other than what follows from the above.
Results may differ from a plain program's by a relative error of at most 0.024.
Values may be sent and summed in bfloat16 or wider, within the bound.
No kernel may reach another device: no remote copies, remote signals or barrier semaphores. Data moves between devices by JAX's collectives and lax.ppermute only.
A program may use at most 64 MiB of HBM per device.

v0:
```python
import jax
import jax.numpy as jnp
from jax import lax
from jax.sharding import PartitionSpec as P

QH = 64
KVH = 8
HD = 128
CACHE = 32
PAGE = 8
QKV = 10240


def rotary_embed(values, positions):
    half = values.shape[-1] // 2
    freqs = 500000.0 ** (-(jnp.arange(half, dtype=jnp.float32) * 2.0) / values.shape[-1])
    angles = positions.astype(jnp.float32)[:, None] * freqs[None, :]
    cosine = jnp.cos(angles)[:, None, :]
    sine = jnp.sin(angles)[:, None, :]
    first = values[..., :half]
    second = values[..., half:]
    return jnp.concatenate(
        [first * cosine - second * sine, second * cosine + first * sine], axis=-1
    )


def regroup(blocks):
    return lax.all_to_all(blocks, "beam", split_axis=1, concat_axis=1, tiled=True)


def attend(queries, fresh_key, value_new, keys, values, positions):
    beams = queries.shape[0]
    grouped_heads = queries.reshape(beams, KVH, QH // KVH, HD)
    scale_factor = HD ** (-0.5)
    scores = (
        jnp.einsum("bkgd,btkd->bkgt", grouped_heads, keys, preferred_element_type=jnp.float32)
        * scale_factor
    )
    local_beam_score = (
        jnp.einsum("rhap,rhp->rha", grouped_heads, fresh_key, preferred_element_type=jnp.float32)
        * scale_factor
    )
    valid = (jnp.arange(keys.shape[1], dtype=jnp.int32)[None, :] < positions[:, None])[
        :, None, None, :
    ]
    scores = jnp.where(valid, scores, -1e30)
    highest = jnp.maximum(jnp.max(scores, axis=-1), local_beam_score)
    weights = jnp.where(valid, jnp.exp(scores - highest[..., None]), 0.0)
    own_weight = jnp.exp(local_beam_score - highest)
    totals = jnp.sum(weights, axis=-1) + own_weight
    probs = (weights / totals[..., None]).astype(jnp.bfloat16)
    own_prob = (own_weight / totals).astype(jnp.bfloat16)
    output = jnp.einsum("bkgt,btkd->bkgd", probs, values, preferred_element_type=jnp.float32)
    output = (
        output
        + own_prob.astype(jnp.float32)[..., None] * value_new.astype(jnp.float32)[:, :, None, :]
    )
    return output.reshape(beams, QH * HD).astype(jnp.bfloat16)


def shards(hidden, norm_gain, w_qkv, w_out, kv_cache, lengths, kept_parent_device, keep_block):
    columns = lax.axis_size("beam")
    my_column = lax.axis_index("beam")
    grouped_row_block = hidden.shape[0]
    own_beams = grouped_row_block // columns
    floats = hidden.astype(jnp.float32)
    scale_rms = lax.rsqrt(jnp.mean(floats * floats, axis=-1, keepdims=True) + 1e-05)
    normed = (floats * scale_rms * norm_gain.astype(jnp.float32)).astype(jnp.bfloat16)
    normed_split = normed.reshape(columns, own_beams, normed.shape[1])
    projected = jnp.einsum(
        "jbd,dc->bjc",
        normed_split,
        lax.all_gather(w_qkv, "owner", axis=0, tiled=True),
        preferred_element_type=jnp.float32,
    )
    own_qkv = regroup(projected.astype(jnp.bfloat16)).reshape(own_beams, QKV)
    blk_dev = kv_cache.shape[0]
    most_slots = max(2, 2 * blk_dev // columns)
    sources = kept_parent_device.reshape(columns, blk_dev)
    picked = keep_block.reshape(columns, blk_dev)
    is_mine = (sources == my_column).astype(jnp.int32)
    ranks = jnp.cumsum(is_mine, axis=1) - 1
    slot_ids = jnp.arange(most_slots, dtype=jnp.int32)
    chosen = is_mine[:, :, None] * (ranks[:, :, None] == slot_ids[None, None, :]).astype(jnp.int32)
    send_table = jnp.sum(chosen * picked[:, :, None], axis=1)
    outgoing = kv_cache[send_table.reshape(-1)].reshape((columns, most_slots) + kv_cache.shape[1:])
    incoming_blocks = lax.all_to_all(outgoing, "beam", split_axis=0, concat_axis=0, tiled=True)
    own_sources = lax.dynamic_index_in_dim(sources, my_column, 0, keepdims=False)
    one_hot = (own_sources[:, None] == jnp.arange(columns, dtype=jnp.int32)[None, :]).astype(
        jnp.int32
    )
    earlier = jnp.cumsum(one_hot, axis=0) - one_hot
    arrival = jnp.sum(earlier * one_hot, axis=1)
    flat_blocks = incoming_blocks.reshape((columns * most_slots,) + kv_cache.shape[1:])
    moved = flat_blocks[own_sources * most_slots + arrival]
    moved = moved.reshape(own_beams, CACHE // PAGE, 2, PAGE, KVH, HD)
    keys = moved[:, :, 0].reshape(own_beams, CACHE, KVH, HD)
    values = moved[:, :, 1].reshape(own_beams, CACHE, KVH, HD)
    positions = lax.dynamic_slice_in_dim(lengths, my_column * own_beams, own_beams)
    query_cols = own_qkv[:, : QH * HD].reshape(own_beams, QH, HD).astype(jnp.float32)
    key_cols = own_qkv[:, QH * HD : (QH + KVH) * HD].reshape(own_beams, KVH, HD).astype(jnp.float32)
    value_new = own_qkv[:, (QH + KVH) * HD :].reshape(own_beams, KVH, HD)
    queries = rotary_embed(query_cols, positions).astype(jnp.bfloat16)
    fresh_key = rotary_embed(key_cols, positions).astype(jnp.bfloat16)
    attn = attend(queries, fresh_key, value_new, keys, values, positions)
    head_rows = regroup(attn.reshape(own_beams, columns, attn.shape[1] // columns))
    w_piece = lax.all_gather(w_out, "owner", axis=1, tiled=True)
    terms = jnp.einsum(
        "bjh,hc->jbc", head_rows, w_piece, preferred_element_type=jnp.float32
    ).reshape(grouped_row_block, w_piece.shape[1])
    return lax.psum_scatter(terms.astype(jnp.bfloat16), "beam", scatter_dimension=1, tiled=True)


def solution(mesh):
    return jax.shard_map(
        shards,
        mesh=mesh,
        in_specs=(
            P("owner", None),
            P(),
            P("owner", "beam"),
            P("beam", "owner"),
            P(("owner", "beam"), None, None, None),
            P("owner"),
            P("owner", None),
            P("owner"),
        ),
        out_specs=P("owner", "beam"),
        check_vma=False,
    )
```

profile of v0, /device:TPU:2, one launch (start us, length us, event | category | flops | bytes accessed | tf_op | source)
XLA Modules:
  0.0 348.0 jit_solution(10896632046652622338)
XLA Ops:
  6.5 0.7 all-gather.3.cloned.1.call-update
  7.3 0.7 all-gather.5.cloned.1.call-update
  8.0 0.5 broadcast.155
  8.5 1.3 reduce.3
  10.0 0.2 reduce_window_sum.22
  10.1 0.8 mul.193
  10.9 0.1 multiply_reduce_fusion
  11.1 0.1 reshape.207
  11.3 2.0 gather_fusion
  13.3 11.7 %all-to-all-start.1 = ((bf16[32,2,2,8,1024]{4,3,2,1,0:T(8,128)(2,1)}), bf16[32,2,2,8,1024]{4,3,2,1,0:T(8,128)(2,1)S(1)}, u32[]{:S(2)}, u32[]{:S(2)}) async-start(bf16[32,2,2,8,1024]{4,3,2,1,0:T(8,128)(2,1)} %bitcast.8), calls=%async_computation.1 | async-start | bytes 4194304 | tf_op jit(solution)/shard_map/all_to_all | solution.py:87
  25.3 0.2 select_reduce_fusion
  25.6 3.1 fusion.1
  28.7 0.1 multiply_cosine_fusion
  28.8 88.1 %all-gather.3.cloned.1.call-done = bf16[8192,320]{0,1:T(8,128)(2,1)} async-done(((bf16[512,320]{0,1:T(8,128)(2,1)}), bf16[8192,320]{0,1:T(8,128)(2,1)}) %all-gather.3.cloned.1.call-update) | async-done | bytes 5242896 | tf_op jit(solution)/shard_map/all_gather | solution.py:73
  116.9 6.8 %fusion.18 = bf16[8,32,320]{2,0,1:T(8,128)(2,1)} fusion(bf16[8192,320]{0,1:T(8,128)(2,1)} %all-gather.3.cloned.1.call-done, bf16[256,8192]{1,0:T(8,128)(2,1)} %param.8, f32[8192]{0:T(1024)S(1)} %convert_element_type.85, f32[256]{0:T(256)S(1)} %add_rsqrt_fusion), kind=kOutput, calls=%fused_computation.21 | convolution fusion | flops 1350647808 | bytes 9634816 | tf_op jit(solution)/shard_map/jbd,dc->bjc/dot_general | solution.py:70
  123.7 10.2 %all-to-all-start = ((bf16[8,32,320]{2,0,1:T(8,128)(2,1)}), bf16[8,32,320]{2,0,1:T(8,128)(2,1)S(1)}, u32[]{:S(2)}, u32[]{:S(2)}) async-start(bf16[8,32,320]{2,0,1:T(8,128)(2,1)} %fusion.18), calls=%async_computation | async-start | bytes 393216 | tf_op jit(solution)/shard_map/all_to_all | solution.py:28
  133.9 1.6 gather_fusion.1
  135.5 1.5 copy.39
  137.2 6.6 %all-to-all-done = bf16[8,32,320]{2,0,1:T(8,128)(2,1)S(1)} async-done(((bf16[8,32,320]{2,0,1:T(8,128)(2,1)}), bf16[8,32,320]{2,0,1:T(8,128)(2,1)S(1)}, u32[]{:S(2)}, u32[]{:S(2)}) %all-to-all-start) | async-done | bytes 163872 | tf_op jit(solution)/shard_map/all_to_all | solution.py:28
  143.8 0.2 reshape.205
  144.3 0.1 fusion.51
  144.4 0.1 fusion.28
  144.5 0.3 fusion.36
  144.8 0.5 fusion.52
  145.3 0.3 fusion.27
  145.6 0.3 fusion.17
  146.0 0.7 copy.32
  146.8 4.3 %all-to-all-start.2 = ((bf16[8,32,256]{2,0,1:T(8,128)(2,1)}), bf16[8,32,256]{2,0,1:T(8,128)(2,1)S(1)}, u32[]{:S(2)}, u32[]{:S(2)}) async-start(bf16[8,32,256]{2,0,1:T(8,128)(2,1)} %copy.32), calls=%async_computation.2 | async-start | bytes 262144 | tf_op jit(solution)/shard_map/all_to_all | solution.py:28
  151.1 58.5 %all-gather.5.cloned.1.call-done = bf16[256,8192]{1,0:T(8,128)(2,1)} async-done(((bf16[256,512]{1,0:T(8,128)(2,1)}), bf16[256,8192]{1,0:T(8,128)(2,1)}) %all-gather.5.cloned.1.call-update) | async-done | bytes 4194320 | tf_op jit(solution)/shard_map/all_gather | solution.py:107
  209.6 3.4 fusion
  213.0 4.2 %copy.67 = bf16[32,8,8192]{2,1,0:T(8,128)(2,1)} copy(bf16[32,8,8192]{2,0,1:T(8,128)(2,1)S(1)} %fusion) | data formatting | bytes 8388608 | tf_op jit(solution)/shard_map/convert_element_type | solution.py:111
  217.3 124.2 %reduce-scatter.2.cloned.1.call-done = bf16[256,256]{1,0:T(8,128)(2,1)} async-done(((bf16[256,8192]{1,0:T(8,128)(2,1)}), bf16[256,256]{1,0:T(8,128)(2,1)}) %reduce-scatter.2.cloned.1.call-update) | async-done | bytes 131088 | tf_op jit(solution)/shard_map/reduce_scatter | solution.py:111
  (38 shorter events, 1.0 us)
Async XLA Ops:
  6.5 4.7 %copy-start = (bf16[32,2,8,1024]{3,2,1,0:T(8,128)(2,1)S(1)}, bf16[32,2,8,1024]{3,2,1,0:T(8,128)(2,1)}, u32[]{:S(2)}) copy-start(bf16[32,2,8,1024]{3,2,1,0:T(8,128)(2,1)} %param.12) | copy-start | bytes 3145732
  6.5 110.3 %all-gather.3.cloned.1.call-start = ((), (), s32[]{:S(2)}) async-start(), calls=%async_computation.4 | async-start | bytes 5570560 | tf_op jit(solution)/shard_map/all_gather | solution.py:73
  7.3 202.3 %all-gather.5.cloned.1.call-start = ((), (), s32[]{:S(2)}) async-start(), calls=%async_computation.5 | async-start | bytes 4456448 | tf_op jit(solution)/shard_map/all_gather | solution.py:107
  11.3 13.8 %copy-start.1 = (bf16[8192]{0:T(1024)(128)(2,1)S(1)}, bf16[8192]{0:T(1024)(128)(2,1)}, u32[]{:S(2)}) copy-start(bf16[8192]{0:T(1024)(128)(2,1)} %param.9) | copy-start | bytes 49156
  11.3 13.9 %copy-start.2 = (s32[256]{0:T(256)S(1)}, s32[256]{0:T(256)}, u32[]{:S(2)}) copy-start(s32[256]{0:T(256)} %param.13) | copy-start | bytes 3076
  13.3 110.4 %all-to-all-start.1 = ((bf16[32,2,2,8,1024]{4,3,2,1,0:T(8,128)(2,1)}), bf16[32,2,2,8,1024]{4,3,2,1,0:T(8,128)(2,1)S(1)}, u32[]{:S(2)}, u32[]{:S(2)}) async-start(bf16[32,2,2,8,1024]{4,3,2,1,0:T(8,128)(2,1)} %bitcast.8), calls=%async_computation.1 | async-start | bytes 4194304 | tf_op jit(solution)/shard_map/all_to_all | solution.py:87
  123.7 20.1 %all-to-all-start = ((bf16[8,32,320]{2,0,1:T(8,128)(2,1)}), bf16[8,32,320]{2,0,1:T(8,128)(2,1)S(1)}, u32[]{:S(2)}, u32[]{:S(2)}) async-start(bf16[8,32,320]{2,0,1:T(8,128)(2,1)} %fusion.18), calls=%async_computation | async-start | bytes 393216 | tf_op jit(solution)/shard_map/all_to_all | solution.py:28
  146.8 62.8 %all-to-all-start.2 = ((bf16[8,32,256]{2,0,1:T(8,128)(2,1)}), bf16[8,32,256]{2,0,1:T(8,128)(2,1)S(1)}, u32[]{:S(2)}, u32[]{:S(2)}) async-start(bf16[8,32,256]{2,0,1:T(8,128)(2,1)} %copy.32), calls=%async_computation.2 | async-start | bytes 262144 | tf_op jit(solution)/shard_map/all_to_all | solution.py:28
  151.0 190.4 %reduce-scatter.2.cloned.1.call-start = ((), (), s32[]{:S(2)}) async-start(), calls=%async_computation.6 | async-start | bytes 4325376 | tf_op jit(solution)/shard_map/reduce_scatter | solution.py:111
Sparse Core Ops, SparseCore 0:
  10.3 106.4 all-gather.2
  119.9 89.6 all-gather.4
  217.4 123.9 reduce-scatter.1
where the time goes:
time: 348 us
  waiting for transfers between devices  279 us (80%)
  starting transfers between devices  26.3 us (8%)
  between operations  13.3 us (4%)
  local copies, waits for them, and re-layouts  12.2 us (4%)
  matrix products  11.4 us (3%)
  other arithmetic  5.99 us (2%)
    reduce_scatter x1, waiting for transfers between devices, shards(): lax.psum_scatter(terms.astype(jnp.bfloat16), 'beam', scatter_dimension=1,...  124 us
    all_gather x1, waiting for transfers between devices, shards(): lax.all_gather(w_qkv, 'owner', axis=0, tiled=True)  88.1 us
    all_gather x1, waiting for transfers between devices, shards(): w_piece = lax.all_gather(w_out, 'owner', axis=1, tiled=True)  58.5 us
    all_to_all x2, starting transfers between devices, regroup(): lax.all_to_all(blocks, 'beam', split_axis=1, concat_axis=1, tiled=True)  14.5 us
    all_to_all x1, starting transfers between devices, shards(): lax.all_to_all(outgoing, 'beam', split_axis=0, concat_axis=0, tiled=True)  11.7 us
  transfers between devices with their start and end apart: 6, of which 4 were waited for; matrix products, arithmetic and copies ran while one was open for 6% of the time, Pallas kernels for 0%

commit v1 on v0

--- a/solution.py
+++ b/solution.py
@@ -70,7 +70,9 @@
     projected = jnp.einsum(
         "jbd,dc->bjc",
         normed_split,
-        lax.all_gather(w_qkv, "owner", axis=0, tiled=True),
+        jnp.concatenate(
+            lax.all_to_all(jnp.stack([w_qkv] * lax.axis_size("owner")), "owner", 0, 0), axis=0
+        ),
         preferred_element_type=jnp.float32,
     )
     own_qkv = regroup(projected.astype(jnp.bfloat16)).reshape(own_beams, QKV)

time: 348 us -> 417 us (1.20)
  waiting for transfers between devices: 279 us -> 320 us
  local copies, waits for them, and re-layouts: 12.2 us -> 32 us
  starting transfers between devices: 26.3 us -> 33.8 us
    all_to_all x0 -> x1, waiting for transfers between devices: none -> 162 us  [shards(): lax.all_to_all(jnp.stack([w_qkv] * lax.axis_size('owner')), 'owner', 0, 0)]
    all_gather x1 -> x0, waiting for transfers between devices: 88.1 us -> none  [shards(): lax.all_gather(w_qkv, 'owner', axis=0, tiled=True)]
    all_gather x1, waiting for transfers between devices: 58.5 us -> 0.02 us  [shards(): w_piece = lax.all_gather(w_out, 'owner', axis=1, tiled=True)]
    all_to_all x1, waiting for transfers between devices: 0.01 us -> 23 us  [shards(): lax.all_to_all(outgoing, 'beam', split_axis=0, concat_axis=0, tiled=True)]
    all_to_all x0 -> x1, starting transfers between devices: none -> 10.4 us  [shards(): lax.all_to_all(jnp.stack([w_qkv] * lax.axis_size('owner')), 'owner', 0, 0)]
    all_to_all x2, waiting for transfers between devices: 6.61 us -> 15.6 us  [regroup(): lax.all_to_all(blocks, 'beam', split_axis=1, concat_axis=1, tiled=True)]
    reshape x0 -> x1, local copies, waits for them, and re-layouts: none -> 8.91 us  [shards(): jnp.concatenate(lax.all_to_all(jnp.stack([w_qkv] * lax.axis_size('owner')...]
    all_to_all x0 -> x1, local copies, waits for them, and re-layouts: none -> 7.77 us  [shards(): lax.all_to_all(jnp.stack([w_qkv] * lax.axis_size('owner')), 'owner', 0, 0)]
  transfers between devices with their start and end apart: 6 -> 6, of which waited for: 4 -> 5; matrix products, arithmetic and copies ran while one was open for 6% -> 9% of each run, Pallas kernels for 0% -> 0%
where the time goes in v1:
time: 417 us; the launch traced here: 416 us
  waiting for transfers between devices  320 us (77%)
  starting transfers between devices  33.8 us (8%)
  local copies, waits for them, and re-layouts  32 us (8%)
  between operations  13.7 us (3%)
  matrix products  11.4 us (3%)
  other arithmetic  5.3 us (1%)
    all_to_all x1, waiting for transfers between devices, shards(): lax.all_to_all(jnp.stack([w_qkv] * lax.axis_size('owner')), 'owner', 0, 0)  162 us
    reduce_scatter x1, waiting for transfers between devices, shards(): lax.psum_scatter(terms.astype(jnp.bfloat16), 'beam', scatter_dimension=1,...  118 us
    all_to_all x1, waiting for transfers between devices, shards(): lax.all_to_all(outgoing, 'beam', split_axis=0, concat_axis=0, tiled=True)  23 us
    all_to_all x2, waiting for transfers between devices, regroup(): lax.all_to_all(blocks, 'beam', split_axis=1, concat_axis=1, tiled=True)  15.6 us
    all_to_all x2, starting transfers between devices, regroup(): lax.all_to_all(blocks, 'beam', split_axis=1, concat_axis=1, tiled=True)  13 us
    all_to_all x1, starting transfers between devices, shards(): lax.all_to_all(jnp.stack([w_qkv] * lax.axis_size('owner')), 'owner', 0, 0)  10.4 us
    all_to_all x1, starting transfers between devices, shards(): lax.all_to_all(outgoing, 'beam', split_axis=0, concat_axis=0, tiled=True)  10.1 us
    reshape x1, local copies, waits for them, and re-layouts, shards(): jnp.concatenate(lax.all_to_all(jnp.stack([w_qkv] * lax.axis_size('owner')...  8.91 us
  transfers between devices with their start and end apart: 6, of which 5 were waited for; matrix products, arithmetic and copies ran while one was open for 9% of the time, Pallas kernels for 0%

profile of v1, /device:TPU:2, one launch (start us, length us, event | category | flops | bytes accessed | tf_op | source)
XLA Modules:
  0.0 415.9 jit_solution(8899453377193502243)
XLA Ops:
  6.5 3.9 stack.2
  10.4 10.4 %all-to-all-start = ((bf16[16,512,320]{1,2,0:T(8,128)(2,1)}), bf16[16,512,320]{1,2,0:T(8,128)(2,1)}, u32[]{:S(2)}, u32[]{:S(2)}) async-start(bf16[16,512,320]{1,2,0:T(8,128)(2,1)} %stack.2), calls=%async_computation | async-start | bytes 10485760 | tf_op jit(solution)/shard_map/all_to_all | solution.py:74
  20.9 0.7 all-gather.2.cloned.1.call-update
  21.6 0.5 broadcast.157
  22.1 0.7 reduce.3
  22.8 0.2 reduce_window_sum.22
  23.5 2.0 gather_fusion
  25.5 162.0 %all-to-all-done = bf16[16,512,320]{1,2,0:T(8,128)(2,1)} async-done(((bf16[16,512,320]{1,2,0:T(8,128)(2,1)}), bf16[16,512,320]{1,2,0:T(8,128)(2,1)}, u32[]{:S(2)}, u32[]{:S(2)}) %all-to-all-start) | async-done | bytes 5242912 | tf_op jit(solution)/shard_map/all_to_all | solution.py:74
  187.5 10.1 %all-to-all-start.2 = ((bf16[32,2,2,8,1024]{4,3,2,1,0:T(8,128)(2,1)}), bf16[32,2,2,8,1024]{4,3,2,1,0:T(8,128)(2,1)S(1)}, u32[]{:S(2)}, u32[]{:S(2)}) async-start(bf16[32,2,2,8,1024]{4,3,2,1,0:T(8,128)(2,1)} %bitcast.7), calls=%async_computation.2 | async-start | bytes 4194304 | tf_op jit(solution)/shard_map/all_to_all | solution.py:89
  197.9 0.2 select_reduce_fusion
  198.1 3.1 fusion.1
  201.4 7.8 %copy.26 = bf16[16,512,320]{1,0,2:T(8,128)(2,1)} copy(bf16[16,512,320]{1,2,0:T(8,128)(2,1)} %all-to-all-done) | data formatting | bytes 10485760 | tf_op jit(solution)/shard_map/all_to_all | solution.py:74
  209.1 8.9 %reshape.236 = bf16[8192,320,1]{0,1,2:T(8,128)(2,1)} reshape(bf16[16,512,320]{1,0,2:T(8,128)(2,1)} %copy.26) | data formatting | bytes 10485760 | tf_op jit(solution)/shard_map/reshape | solution.py:73
  218.1 6.8 %fusion.15 = bf16[8,32,320]{2,0,1:T(8,128)(2,1)} fusion(bf16[8192,320,1]{0,1,2:T(8,128)(2,1)} %reshape.236, bf16[256,8192]{1,0:T(8,128)(2,1)} %param.8, f32[8192]{0:T(1024)S(1)} %convert_element_type.85, f32[256]{0:T(256)S(1)} %add_rsqrt_fusion), kind=kOutput, calls=%fused_computation.20 | convolution fusion | flops 1350647808 | bytes 9634816 | tf_op jit(solution)/shard_map/jbd,dc->bjc/dot_general | solution.py:70
  224.9 23.0 %all-to-all-done.2 = bf16[32,2,2,8,1024]{4,3,2,1,0:T(8,128)(2,1)S(1)} async-done(((bf16[32,2,2,8,1024]{4,3,2,1,0:T(8,128)(2,1)}), bf16[32,2,2,8,1024]{4,3,2,1,0:T(8,128)(2,1)S(1)}, u32[]{:S(2)}, u32[]{:S(2)}) %all-to-all-start.2) | async-done | bytes 2097184 | tf_op jit(solution)/shard_map/all_to_all | solution.py:89
  247.9 8.8 %all-to-all-start.1 = ((bf16[8,32,320]{2,0,1:T(8,128)(2,1)}), bf16[8,32,320]{2,0,1:T(8,128)(2,1)S(1)}, u32[]{:S(2)}, u32[]{:S(2)}) async-start(bf16[8,32,320]{2,0,1:T(8,128)(2,1)} %fusion.15), calls=%async_computation.1 | async-start | bytes 393216 | tf_op jit(solution)/shard_map/all_to_all | solution.py:28
  256.7 1.6 gather_fusion.1
  258.3 1.5 copy.41
  259.9 6.7 %all-to-all-done.1 = bf16[8,32,320]{2,0,1:T(8,128)(2,1)S(1)} async-done(((bf16[8,32,320]{2,0,1:T(8,128)(2,1)}), bf16[8,32,320]{2,0,1:T(8,128)(2,1)S(1)}, u32[]{:S(2)}, u32[]{:S(2)}) %all-to-all-start.1) | async-done | bytes 163872 | tf_op jit(solution)/shard_map/all_to_all | solution.py:28
  266.6 0.2 reshape.211
  267.0 0.1 fusion.46
  267.3 0.3 fusion.31
  267.5 0.5 fusion.47
  268.1 0.3 fusion.22
  268.4 0.3 fusion.14
  268.8 0.7 copy.34
  269.5 4.3 %all-to-all-start.3 = ((bf16[8,32,256]{2,0,1:T(8,128)(2,1)}), bf16[8,32,256]{2,0,1:T(8,128)(2,1)S(1)}, u32[]{:S(2)}, u32[]{:S(2)}) async-start(bf16[8,32,256]{2,0,1:T(8,128)(2,1)} %copy.34), calls=%async_computation.3 | async-start | bytes 262144 | tf_op jit(solution)/shard_map/all_to_all | solution.py:28
  273.8 0.2 reduce-scatter.2.cloned.1.call-start
  274.0 8.9 %all-to-all-done.3 = bf16[8,32,256]{2,0,1:T(8,128)(2,1)S(1)} async-done(((bf16[8,32,256]{2,0,1:T(8,128)(2,1)}), bf16[8,32,256]{2,0,1:T(8,128)(2,1)S(1)}, u32[]{:S(2)}, u32[]{:S(2)}) %all-to-all-start.3) | async-done | bytes 131104 | tf_op jit(solution)/shard_map/all_to_all | solution.py:28
  282.9 3.4 fusion
  286.4 4.2 %copy.69 = bf16[32,8,8192]{2,1,0:T(8,128)(2,1)} copy(bf16[32,8,8192]{2,0,1:T(8,128)(2,1)S(1)} %fusion) | data formatting | bytes 8388608 | tf_op jit(solution)/shard_map/convert_element_type | solution.py:113
  290.6 118.4 %reduce-scatter.2.cloned.1.call-done = bf16[256,256]{1,0:T(8,128)(2,1)} async-done(((bf16[256,8192]{1,0:T(8,128)(2,1)}), bf16[256,256]{1,0:T(8,128)(2,1)}) %reduce-scatter.2.cloned.1.call-update) | async-done | bytes 131088 | tf_op jit(solution)/shard_map/reduce_scatter | solution.py:113
  (44 shorter events, 1.5 us)
Async XLA Ops:
  6.5 16.9 %copy-start = (bf16[32,2,8,1024]{3,2,1,0:T(8,128)(2,1)S(1)}, bf16[32,2,8,1024]{3,2,1,0:T(8,128)(2,1)}, u32[]{:S(2)}) copy-start(bf16[32,2,8,1024]{3,2,1,0:T(8,128)(2,1)} %param.12) | copy-start | bytes 3145732
  10.4 11.6 %copy-start.3 = (s32[1024,1]{0,1:T(1,128)S(1)}, s32[1024,1]{0,1:T(1,128)}, u32[]{:S(2)}) copy-start(s32[1024,1]{0,1:T(1,128)} %param.14) | copy-start | bytes 12292
  10.4 12.6 %copy-start.2 = (s32[1024]{0:T(1024)S(1)}, s32[1024]{0:T(1024)}, u32[]{:S(2)}) copy-start(s32[1024]{0:T(1024)} %param.15) | copy-start | bytes 12292
  10.4 177.0 %all-to-all-start = ((bf16[16,512,320]{1,2,0:T(8,128)(2,1)}), bf16[16,512,320]{1,2,0:T(8,128)(2,1)}, u32[]{:S(2)}, u32[]{:S(2)}) async-start(bf16[16,512,320]{1,2,0:T(8,128)(2,1)} %stack.2), calls=%async_computation | async-start | bytes 10485760 | tf_op jit(solution)/shard_map/all_to_all | solution.py:74
  20.8 253.2 %all-gather.2.cloned.1.call-start = ((), (), s32[]{:S(2)}) async-start(), calls=%async_computation.5 | async-start | bytes 4456448 | tf_op jit(solution)/shard_map/all_gather | solution.py:109
  23.4 174.2 %copy-start.1 = (bf16[8192]{0:T(1024)(128)(2,1)S(1)}, bf16[8192]{0:T(1024)(128)(2,1)}, u32[]{:S(2)}) copy-start(bf16[8192]{0:T(1024)(128)(2,1)} %param.9) | copy-start | bytes 49156
  23.5 174.3 %copy-start.4 = (s32[256]{0:T(256)S(1)}, s32[256]{0:T(256)}, u32[]{:S(2)}) copy-start(s32[256]{0:T(256)} %param.13) | copy-start | bytes 3076
  187.5 60.4 %all-to-all-start.2 = ((bf16[32,2,2,8,1024]{4,3,2,1,0:T(8,128)(2,1)}), bf16[32,2,2,8,1024]{4,3,2,1,0:T(8,128)(2,1)S(1)}, u32[]{:S(2)}, u32[]{:S(2)}) async-start(bf16[32,2,2,8,1024]{4,3,2,1,0:T(8,128)(2,1)} %bitcast.7), calls=%async_computation.2 | async-start | bytes 4194304 | tf_op jit(solution)/shard_map/all_to_all | solution.py:89
  247.9 18.6 %all-to-all-start.1 = ((bf16[8,32,320]{2,0,1:T(8,128)(2,1)}), bf16[8,32,320]{2,0,1:T(8,128)(2,1)S(1)}, u32[]{:S(2)}, u32[]{:S(2)}) async-start(bf16[8,32,320]{2,0,1:T(8,128)(2,1)} %fusion.15), calls=%async_computation.1 | async-start | bytes 393216 | tf_op jit(solution)/shard_map/all_to_all | solution.py:28
  269.5 13.4 %all-to-all-start.3 = ((bf16[8,32,256]{2,0,1:T(8,128)(2,1)}), bf16[8,32,256]{2,0,1:T(8,128)(2,1)S(1)}, u32[]{:S(2)}, u32[]{:S(2)}) async-start(bf16[8,32,256]{2,0,1:T(8,128)(2,1)} %copy.34), calls=%async_computation.3 | async-start | bytes 262144 | tf_op jit(solution)/shard_map/all_to_all | solution.py:28
  273.8 135.3 %reduce-scatter.2.cloned.1.call-start = ((), (), s32[]{:S(2)}) async-start(), calls=%async_computation.6 | async-start | bytes 4325376 | tf_op jit(solution)/shard_map/reduce_scatter | solution.py:113
Sparse Core Ops, SparseCore 0:
  24.6 162.0 all-gather.1
  290.8 118.2 reduce-scatter.1
